TPU v7x, 512 devices: a whole 4x4x16 slice. The times are simulated.
512 devices in a mesh: req: 32 (over y, x, core), grp: 16 (over z).
Axes of the slice: x: 4, y: 4, z: 16, core: 2. Of those that a mesh axis runs over, the one named last changes fastest.
Arguments:
- normed_token_input: bfloat16 [256, 8192], P(None, 'req'), may hold values from -6 to 6
- key_value_weight: bfloat16 [8192, 2048], P('req', 'grp'), may hold values from -0.0625 to 0.0625
- adapter_down_weight: bfloat16 [8192, 128, 128], P('req', 'grp'), may hold values from -0.0625 to 0.0625
- adapter_up_weight: bfloat16 [128, 64, 2048], P(None, None, 'grp'), may hold values from -0.75 to 0.75
- adapter_index_rows: int32 [256, 1], replicated, may hold values from 0 to 127
- queries: bfloat16 [256, 8192], P('req')
- key_value_pages: bfloat16 [10240, 16, 2, 8, 128], P('req', 'grp')
- lengths: int32 [256], P('req'), may hold values from 0 to 511, as said below
- page_slot_table: int32 [256, 32], P('req'), may hold values from 0 to 255, as said below
- departing_slots: int32 [1024], P('req'), may hold values from 0 to 255, as said below
- departing_target: int32 [1024, 1], P('req'), may hold values from 0 to 31; in each aligned block of 32 rows (0 to 31, 32 to 63, ...) at most 2 rows name the same one
Outputs:
- attention: bfloat16 [256, 8192], P('req')
- migrated_pool: bfloat16 [10240, 16, 2, 8, 128], P('req', 'grp')
Inputs may be any that keep to these rules, and one draw needn't show every extreme that they name: `adapter_index_rows`: each row names one adapter; every adapter is named by some request. `lengths`: some request has an empty cache and some has 511 cached tokens. `page_slot_table`: the rows of the requests of one home together name each of that home's slots 0 .. 255 exactly once. `departing_slots`: the 32 entries of one home are distinct. `departing_target`: the 32 rows of one home name one target at most 2 times; some home names some target exactly 2 times.
All inputs are finite; a program needn't handle non-finite values.
Results may differ from a plain program's by a relative error of at most 0.01345.
Values may be sent and summed in bfloat16 or wider, within the bound.
No kernel may reach another device: no remote copies, remote signals or barrier semaphores. Data moves between devices by JAX's collectives and lax.ppermute only.
A program may use at most 64 MiB of HBM per device.

v0:
```python
import math
import jax
import jax.numpy as jnp
from jax import lax
from jax.sharding import PartitionSpec as P

adapter_scale = 2.0
masked_score = -1e30


def shards(
    normed_token_input,
    key_value_weight,
    adapter_down_weight,
    adapter_up_weight,
    adapter_index_rows,
    queries,
    key_value_pages,
    lengths,
    page_slot_table,
    departing_slots,
    departing_target,
):
    selected_adapter = adapter_index_rows[:, 0]
    homes = lax.axis_size("req")
    groups = lax.axis_size("grp")
    home_index = lax.axis_index("req")
    group_index = lax.axis_index("grp")
    rows = lengths.shape[0]
    request_count = normed_token_input.shape[0]
    column_span = key_value_weight.shape[1]
    local_adapters = adapter_down_weight.shape[1]
    rank_width = adapter_down_weight.shape[2]
    rank_half = adapter_up_weight.shape[1]
    slot_tokens = key_value_pages.shape[1]
    heads = key_value_pages.shape[3]
    head_dim = key_value_pages.shape[4]
    key_width = heads * head_dim
    query_heads = queries.shape[1] // head_dim
    heads_per_target = query_heads // groups
    page_size = slot_tokens * groups
    pages = page_slot_table.shape[1]
    both = jnp.concatenate(
        [key_value_weight, adapter_down_weight.reshape(adapter_down_weight.shape[0], -1)], axis=1
    )
    products = jnp.dot(normed_token_input, both, preferred_element_type=jnp.float32)
    base_part = products[:, :column_span]
    down_all = products[:, column_span:].reshape(request_count, local_adapters, rank_width)
    local_choice = selected_adapter - group_index * local_adapters
    picker = (local_choice[:, None] == jnp.arange(local_adapters, dtype=jnp.int32)[None, :]).astype(
        jnp.float32
    )
    mid_part = jnp.einsum("ia,iaw->iw", picker, down_all)
    partial = jnp.concatenate([base_part, mid_part], axis=1).reshape(homes, rows, -1)
    summed = jnp.sum(lax.all_to_all(partial, "req", 0, 0, tiled=False), axis=0)
    base_resident = summed[:, :column_span]
    mid_owned = summed[:, column_span:].astype(jnp.bfloat16)
    resident_adapters = lax.dynamic_slice_in_dim(selected_adapter, home_index * rows, rows)
    owner = resident_adapters // local_adapters
    mid_spread = lax.all_to_all(
        jnp.broadcast_to(mid_owned[None], (groups,) + mid_owned.shape), "grp", 0, 0, tiled=False
    )
    request_index = jnp.arange(rows, dtype=jnp.int32)
    mid_home = mid_spread[owner, request_index]
    is_value = group_index * column_span >= key_width
    mid_used = jnp.where(is_value, mid_home[:, rank_half:], mid_home[:, :rank_half])
    up_weight_rows = adapter_up_weight[resident_adapters]
    adapter_update = jnp.einsum(
        "ir,irc->ic", mid_used, up_weight_rows, preferred_element_type=jnp.float32
    )
    fresh_columns = (base_resident + adapter_scale * adapter_update).astype(jnp.bfloat16)
    gathered = key_value_pages[page_slot_table][:, :, 0]
    keys = gathered[:, :, 0]
    values = gathered[:, :, 1]
    query = queries.reshape(rows, heads, -1, head_dim)
    scores = jnp.einsum(
        "ihgd,inhd->ihgn", query, keys, preferred_element_type=jnp.float32
    ) / math.sqrt(head_dim)
    positions = jnp.arange(pages, dtype=jnp.int32) * page_size + group_index * slot_tokens
    valid = (positions[None, :] < lengths[:, None])[:, None, None, :]
    scores = jnp.where(valid, scores, masked_score)
    local_top = jnp.max(scores, axis=3)
    weights = jnp.where(valid, jnp.exp(scores - local_top[..., None]), 0.0)
    local_total = jnp.sum(weights, axis=3)
    local_mixed = jnp.einsum("ihgn,inhd->ihgd", weights, values, preferred_element_type=jnp.float32)
    parcel = jnp.concatenate(
        [
            local_mixed.reshape(rows, groups, heads_per_target * head_dim),
            local_top.reshape(rows, groups, heads_per_target),
            local_total.reshape(rows, groups, heads_per_target),
            jnp.broadcast_to(
                fresh_columns.astype(jnp.float32)[:, None, :], (rows, groups, column_span)
            ),
        ],
        axis=2,
    ).transpose(1, 0, 2)
    received = lax.all_to_all(parcel, "grp", 0, 0, tiled=False)
    mixed_width = heads_per_target * head_dim
    shard_mixed = received[:, :, :mixed_width].reshape(groups, rows, heads_per_target, head_dim)
    shard_top = received[:, :, mixed_width : mixed_width + heads_per_target]
    shard_total = received[
        :, :, mixed_width + heads_per_target : mixed_width + 2 * heads_per_target
    ]
    new_all = received[:, :, mixed_width + 2 * heads_per_target :].astype(jnp.bfloat16)
    new_all = new_all.transpose(1, 0, 2).reshape(rows, groups * column_span)
    new_keys = new_all[:, :key_width].reshape(rows, heads, head_dim)
    new_values = new_all[:, key_width:].reshape(rows, heads, head_dim)
    head_of_target = group_index * heads_per_target // (query_heads // heads)
    own_query = lax.dynamic_slice_in_dim(
        queries, group_index * mixed_width, mixed_width, axis=1
    ).reshape(rows, heads_per_target, head_dim)
    own_key = lax.dynamic_index_in_dim(new_keys, head_of_target, 1, False)
    own_value = lax.dynamic_index_in_dim(new_values, head_of_target, 1, False)
    new_score = jnp.einsum(
        "ihd,id->ih", own_query, own_key, preferred_element_type=jnp.float32
    ) / math.sqrt(head_dim)
    top = jnp.maximum(jnp.max(shard_top, axis=0), new_score)
    shard_scale = jnp.exp(shard_top - top[None])
    new_weight = jnp.exp(new_score - top)
    total = jnp.sum(shard_total * shard_scale, axis=0) + new_weight
    mixed = (
        jnp.sum(shard_mixed * shard_scale[..., None], axis=0)
        + new_weight[..., None] * own_value.astype(jnp.float32)[:, None, :]
    )
    own_attention = (mixed / total[..., None]).astype(jnp.bfloat16).reshape(rows, mixed_width)
    attention = lax.all_gather(own_attention, "grp", axis=1, tiled=True)
    page_slot = page_slot_table[request_index, lengths // page_size]
    offset = lengths % page_size
    mine = offset // slot_tokens == group_index
    token_local = offset % slot_tokens
    current = key_value_pages[page_slot, token_local]
    fresh = jnp.stack([new_keys, new_values], axis=1)
    written = key_value_pages.at[page_slot, token_local].set(
        jnp.where(mine[:, None, None, None], fresh, current)
    )
    targets = departing_target[:, 0]
    count_out = departing_slots.shape[0]
    order = jnp.arange(count_out, dtype=jnp.int32)
    earlier = (targets[:, None] == targets[None, :]) & (order[None, :] < order[:, None])
    place = jnp.sum(earlier.astype(jnp.int32), axis=1)
    live_slots = rows * pages
    capacity = (key_value_pages.shape[0] - live_slots) // homes
    outbound = (
        jnp.zeros((homes, capacity) + key_value_pages.shape[1:], key_value_pages.dtype)
        .at[targets, place]
        .set(written[departing_slots])
    )
    arrived = lax.all_to_all(outbound, "req", split_axis=0, concat_axis=0, tiled=True)
    migrated_pool = jnp.concatenate(
        [written[:live_slots], arrived.reshape((homes * capacity,) + key_value_pages.shape[1:])],
        axis=0,
    )
    return (attention, migrated_pool)


def solution(mesh):
    in_specs = (
        P(None, "req"),
        P("req", "grp"),
        P("req", "grp", None),
        P(None, None, "grp"),
        P(),
        P("req", None),
        P("req", "grp", None, None, None),
        P("req"),
        P("req", None),
        P("req"),
        P("req", None),
    )
    out_specs = (P("req", None), P("req", "grp", None, None, None))
    return jax.shard_map(shards, mesh=mesh, in_specs=in_specs, out_specs=out_specs, check_vma=False)
```

profile of v0, /device:TPU:1, one launch (start us, length us, event | category | flops | bytes accessed | tf_op | source)
XLA Modules:
  0.0 158.4 jit_solution(13711185269570245694)
XLA Ops:
  0.7 1.5 copy.92
  2.4 0.4 convolution_bitcast_fusion
  2.8 1.1 slice.84
  3.9 0.2 copy-done.2
  4.1 0.8 fusion.11
  4.9 1.0 copy.63
  5.8 1.3 multiply_reduce_fusion
  7.2 0.7 pad_maximum_fusion.1
  7.9 1.8 %copy.43 = f32[256,256]{1,0:T(8,128)} copy(f32[256,256]{0,1:T(8,128)} %pad_maximum_fusion.1) | data formatting | bytes 524288 | tf_op jit(solution)/shard_map/concatenate | solution.py:54
  9.7 11.0 %all-to-all-start = ((f32[32,8,256]{2,1,0:T(8,128)}), f32[32,8,256]{2,1,0:T(8,128)}, u32[]{:S(2)}, u32[]{:S(2)}) async-start(f32[32,8,256]{2,1,0:T(8,128)} %bitcast.113), calls=%async_computation | async-start | bytes 524288 | tf_op jit(solution)/shard_map/all_to_all | solution.py:55
  20.8 1.8 %gather_fusion = bf16[256,2,8,128]{3,2,1,0:T(8,128)(2,1)} fusion(bf16[320,2,8,128]{3,2,1,0:T(8,128)(2,1)S(1)} %bitcast.107, s32[1024]{0:T(1024)S(1)} %pad_clamp_fusion.2), kind=kCustom, calls=%fused_computation | custom fusion | bytes 2098176 | tf_op jit(solution)/shard_map/gather | solution.py:72
  22.6 2.1 %fusion.41 = (bf16[8,32,1,8,128]{4,3,2,1,0:T(8,128)(2,1)}, bf16[8,32,1,8,128]{4,3,2,1,0:T(8,128)(2,1)S(1)}) fusion(bf16[8,32,2,8,128]{4,3,2,1,0:T(8,128)(2,1)} %bitcast.110), kind=kLoop, calls=%fused_computation.114 | loop fusion | bytes 2097152 | tf_op jit(solution)/shard_map/slice | solution.py:74
  24.8 0.5 fusion.42
  25.3 0.7 copy-done.3
  26.0 0.3 fusion.7
  26.2 2.1 %fusion.5 = f32[8,8,8,128]{3,2,1,0:T(8,128)} fusion(bf16[8,32,1,8,128]{4,3,2,1,0:T(8,128)(2,1)} %get-tuple-element.6, f32[8,8,8,32]{3,2,1,0:T(8,128)} %copy-done.3, f32[8,8,8]{2,1,0:T(8,128)S(1)} %get-tuple-element.16, pred[8,32]{1,0:T(8,128)(4,1)S(1)} %broadcast_compare_fusion), kind=kOutput, calls=%fused_computation.20 | convolution fusion | flops 4227072 | bytes 854272 | tf_op jit(solution)/shard_map/ihgn,inhd->ihgd/dot_general | solution.py:85
  28.4 1.4 all-to-all-done
  29.8 1.0 reduce_sum.48
  30.7 0.6 broadcast_in_dim.45
  31.4 12.5 %all-to-all-start.1 = ((bf16[16,8,128]{2,1,0:T(8,128)(2,1)}), bf16[16,8,128]{2,1,0:T(8,128)(2,1)}, u32[]{:S(2)}, u32[]{:S(2)}) async-start(bf16[16,8,128]{2,1,0:T(8,128)(2,1)} %broadcast_in_dim.45), calls=%async_computation.1 | async-start | bytes 65536 | tf_op jit(solution)/shard_map/all_to_all | solution.py:60
  43.9 0.6 fusion.35
  44.5 0.7 copy.41
  45.3 0.2 copy.46
  45.4 0.9 copy.45
  46.4 1.7 %reshape.115 = f32[8,16,512]{2,1,0:T(8,128)} reshape(f32[8,8,8,128]{3,2,1,0:T(8,128)} %fusion.5) | data formatting | bytes 524288 | tf_op jit(solution)/shard_map/reshape | solution.py:88
  48.0 1.8 %copy.44 = f32[8,16,512]{2,0,1:T(8,128)} copy(f32[8,16,512]{2,1,0:T(8,128)} %reshape.115) | data formatting | bytes 524288 | tf_op jit(solution)/shard_map/reshape | solution.py:88
  49.8 1.2 pad_clamp_fusion.1
  51.1 1.3 gather_fusion.2
  52.4 3.1 %all-to-all-done.1 = bf16[16,8,128]{2,1,0:T(8,128)(2,1)} async-done(((bf16[16,8,128]{2,1,0:T(8,128)(2,1)}), bf16[16,8,128]{2,1,0:T(8,128)(2,1)}, u32[]{:S(2)}, u32[]{:S(2)}) %all-to-all-start.1) | async-done | bytes 32800 | tf_op jit(solution)/shard_map/all_to_all | solution.py:60
  55.5 1.9 %gather_fusion.1 = bf16[8,128]{1,0:T(8,128)(2,1)} fusion(bf16[16,8,128]{2,1,0:T(8,128)(2,1)} %all-to-all-done.1, s32[8]{0:T(128)S(1)} %get-tuple-element.12), kind=kCustom, calls=%fused_computation.1 | custom fusion | bytes 4160 | tf_op jit(solution)/shard_map/gather | solution.py:64
  57.4 0.8 select_bitcast_fusion
  58.2 1.0 fusion.20
  59.3 1.8 %maximum_bitcast_fusion = f32[16,8,648]{2,1,0:T(8,128)} fusion(f32[8,16,128]{2,0,1:T(8,128)S(1)} %broadcast_in_dim.46, f32[8,16,4]{2,0,1:T(8,128)S(1)} %copy.46, f32[8,16,4]{2,0,1:T(8,128)S(1)} %copy.45, f32[8,16,512]{2,0,1:T(8,128)} %copy.44), kind=kLoop, calls=%fused_computation.22 | loop fusion | flops 248832 | bytes 663552 | tf_op jit(solution)/shard_map/transpose | solution.py:96
  61.1 8.4 %all-to-all-start.2 = ((f32[16,8,648]{2,1,0:T(8,128)}), f32[16,8,648]{2,1,0:T(8,128)}, u32[]{:S(2)}, u32[]{:S(2)}) async-start(f32[16,8,648]{2,1,0:T(8,128)} %maximum_bitcast_fusion), calls=%async_computation.2 | async-start | bytes 786432 | tf_op jit(solution)/shard_map/all_to_all | solution.py:97
  69.5 0.7 fusion.34
  70.2 0.6 gather_fusion.3
  70.8 0.6 shift-left_bitcast_fusion
  71.4 0.6 gather_fusion.4
  72.0 0.7 compare_select_fusion.1
  72.7 0.6 pad_clamp_fusion
  73.3 0.7 dynamic-slice_bitcast_fusion
  74.0 0.9 convert_reduce_fusion
  74.9 1.2 fusion.26
  76.1 0.7 fusion.36
  76.7 10.9 %all-to-all-done.2 = f32[16,8,648]{2,1,0:T(8,128)} async-done(((f32[16,8,648]{2,1,0:T(8,128)}), f32[16,8,648]{2,1,0:T(8,128)}, u32[]{:S(2)}, u32[]{:S(2)}) %all-to-all-start.2) | async-done | bytes 331808 | tf_op jit(solution)/shard_map/all_to_all | solution.py:97
  87.7 1.0 fusion.14
  88.7 0.6 slice_bitcast_fusion.3
  89.4 0.9 slice_reduce_fusion
  90.3 1.0 fusion.13
  91.3 0.2 copy.47
  91.6 0.7 bitcast_convert_fusion
  92.3 1.1 fusion.6
  93.5 28.5 %all_gather.3 = bf16[8,8192]{1,0:T(8,128)(2,1)} all-gather(bf16[8,512]{1,0:T(8,128)(2,1)S(1)} %fusion.15), channel_id=1, replica_groups=mesh['req'=32,'grp'=16] {'grp'}, dimensions={1}, use_global_device_ids=true | all-gather | bytes 139264 | tf_op jit(solution)/shard_map/all_gather | solution.py:126
  122.0 0.7 copy_bitcast_fusion.5
  122.7 0.7 maximum_select_fusion
  123.4 0.8 scatter_fusion
  124.3 0.7 gather_fusion.5
  125.0 0.7 broadcast.228
  125.7 3.8 %scatter_fusion.1 = bf16[32,2,2,8,128]{4,3,2,1,0:T(8,128)(2,1)} fusion(bf16[32,2,2,8,128]{4,3,2,1,0:T(8,128)(2,1)} %broadcast.228, s32[32]{0:T(128)S(1)} %fusion.36, bf16[32,2,8,128]{3,2,1,0:T(8,128)(2,1)S(1)} %gather_fusion.5), kind=kCustom, calls=%fused_computation.7 | custom fusion | bytes 393472 | tf_op jit(solution)/shard_map/scatter | solution.py:146
  129.5 16.8 %all-to-all-start.3 = ((bf16[32,2,1,2,8,128]{5,4,3,1,2,0:T(8,128)(2,1)}), bf16[32,2,1,2,8,128]{5,4,3,1,2,0:T(8,128)(2,1)}, u32[]{:S(2)}, u32[]{:S(2)}) async-start(bf16[32,2,1,2,8,128]{5,4,3,1,2,0:T(8,128)(2,1)} %bitcast.112), calls=%async_computation.3 | async-start | bytes 524288 | tf_op jit(solution)/shard_map/all_to_all | solution.py:148
  146.3 1.2 slice_bitcast_fusion
  147.4 7.8 %all-to-all-done.3 = bf16[32,2,1,2,8,128]{5,4,3,1,2,0:T(8,128)(2,1)} async-done(((bf16[32,2,1,2,8,128]{5,4,3,1,2,0:T(8,128)(2,1)}), bf16[32,2,1,2,8,128]{5,4,3,1,2,0:T(8,128)(2,1)}, u32[]{:S(2)}, u32[]{:S(2)}) %all-to-all-start.3) | async-done | bytes 262176 | tf_op jit(solution)/shard_map/all_to_all | solution.py:148
  155.2 2.5 %pad_maximum_fusion = bf16[320,1,2,8,128]{4,3,2,1,0:T(8,128)(2,1)} fusion(bf16[64,1,2,8,128]{4,3,2,1,0:T(8,128)(2,1)} %bitcast.43, bf16[256,1,2,8,128]{4,3,2,1,0:T(8,128)(2,1)} %slice_bitcast_fusion), kind=kLoop, calls=%fused_computation.9 | loop fusion | flops 655360 | bytes 2621440 | tf_op jit(solution)/shard_map/concatenate | solution.py:149
  157.7 0.7 copy.93
  (42 shorter events, 0.9 us)
Async XLA Ops:
  0.6 50.4 %copy-start = (bf16[128,64,128]{2,1,0:T(8,128)(2,1)S(1)}, bf16[128,64,128]{2,1,0:T(8,128)(2,1)}, u32[]{:S(2)}) copy-start(bf16[128,64,128]{2,1,0:T(8,128)(2,1)} %param.14) | copy-start | bytes 6291460
  0.6 1.7 %copy-start.6 = (bf16[256,256]{1,0:T(8,128)(2,1)S(1)}, bf16[256,256]{1,0:T(8,128)(2,1)}, u32[]{:S(2)}) copy-start(bf16[256,256]{1,0:T(8,128)(2,1)} %param.11) | copy-start | bytes 393220
  0.7 1.7 %copy-start.7 = (bf16[256,128]{1,0:T(8,128)(2,1)S(1)}, bf16[256,128]{1,0:T(8,128)(2,1)}, u32[]{:S(2)}) copy-start(bf16[256,128]{1,0:T(8,128)(2,1)} %param.12) | copy-start | bytes 196612
  0.7 1.6 %copy-start.4 = (bf16[256,8,128]{2,1,0:T(8,128)(2,1)S(1)}, bf16[256,8,128]{2,1,0:T(8,128)(2,1)}, u32[]{:S(2)}) copy-start(bf16[256,8,128]{2,1,0:T(8,128)(2,1)} %param.13) | copy-start | bytes 1572868
  2.7 1.4 copy-start.2
  2.8 1.4 copy-start.8
  4.1 3.1 %slice-start = ((f32[256,1152]{0,1:T(8,128)}), f32[256,128]{0,1:T(8,128)S(1)}, s32[]{:S(2)}) async-start(f32[256,1152]{0,1:T(8,128)} %copy-done.2), calls=%async_computation.4 | async-start | bytes 262144 | tf_op jit(solution)/shard_map/slice | solution.py:47
  5.8 14.9 %copy-start.1 = (s32[8,32]{1,0:T(8,128)S(1)}, s32[8,32]{1,0:T(8,128)}, u32[]{:S(2)}) copy-start(s32[8,32]{1,0:T(8,128)} %param.19) | copy-start | bytes 3076
  9.7 20.1 %all-to-all-start = ((f32[32,8,256]{2,1,0:T(8,128)}), f32[32,8,256]{2,1,0:T(8,128)}, u32[]{:S(2)}, u32[]{:S(2)}) async-start(f32[32,8,256]{2,1,0:T(8,128)} %bitcast.113), calls=%async_computation | async-start | bytes 524288 | tf_op jit(solution)/shard_map/all_to_all | solution.py:55
  22.6 2.1 %copy-start.11 = (s32[8]{0:T(128)S(1)}, s32[8]{0:T(128)}, u32[]{:S(2)}) copy-start(s32[8]{0:T(128)} %param.18) | copy-start | bytes 100
  22.6 2.2 %copy-start.10 = (bf16[8,8192]{1,0:T(8,128)(2,1)S(1)}, bf16[8,8192]{1,0:T(8,128)(2,1)}, u32[]{:S(2)}) copy-start(bf16[8,8192]{1,0:T(8,128)(2,1)} %param.16) | copy-start | bytes 393220
  24.8 19.1 %copy-start.9 = (s32[256,1]{0,1:T(1,128)S(1)}, s32[256,1]{0,1:T(1,128)}, u32[]{:S(2)}) copy-start(s32[256,1]{0,1:T(1,128)} %param.15) | copy-start | bytes 3076
  25.3 0.7 copy-start.3
  31.4 24.1 %all-to-all-start.1 = ((bf16[16,8,128]{2,1,0:T(8,128)(2,1)}), bf16[16,8,128]{2,1,0:T(8,128)(2,1)}, u32[]{:S(2)}, u32[]{:S(2)}) async-start(bf16[16,8,128]{2,1,0:T(8,128)(2,1)} %broadcast_in_dim.45), calls=%async_computation.1 | async-start | bytes 65536 | tf_op jit(solution)/shard_map/all_to_all | solution.py:60
  61.1 26.6 %all-to-all-start.2 = ((f32[16,8,648]{2,1,0:T(8,128)}), f32[16,8,648]{2,1,0:T(8,128)}, u32[]{:S(2)}, u32[]{:S(2)}) async-start(f32[16,8,648]{2,1,0:T(8,128)} %maximum_bitcast_fusion), calls=%async_computation.2 | async-start | bytes 786432 | tf_op jit(solution)/shard_map/all_to_all | solution.py:97
  129.5 25.7 %all-to-all-start.3 = ((bf16[32,2,1,2,8,128]{5,4,3,1,2,0:T(8,128)(2,1)}), bf16[32,2,1,2,8,128]{5,4,3,1,2,0:T(8,128)(2,1)}, u32[]{:S(2)}, u32[]{:S(2)}) async-start(bf16[32,2,1,2,8,128]{5,4,3,1,2,0:T(8,128)(2,1)} %bitcast.112), calls=%async_computation.3 | async-start | bytes 524288 | tf_op jit(solution)/shard_map/all_to_all | solution.py:148
  155.2 2.5 %copy-start.5 = (bf16[8,8192]{1,0:T(8,128)(2,1)S(1)}, bf16[8,8192]{1,0:T(8,128)(2,1)}, u32[]{:S(2)}) copy-start(bf16[8,8192]{1,0:T(8,128)(2,1)} %all_gather.3) | copy-start | bytes 393220
where the time goes:
time: 160 us; the launch traced here: 158 us
  starting transfers between devices  48.7 us (30%)
  local copies, waits for them, and re-layouts  32.1 us (20%)
  blocking collectives  28.5 us (18%)
  waiting for transfers between devices  23.2 us (14%)
  other arithmetic  20.9 us (13%)
  matrix products  4.13 us (3%)
    all_gather x1, blocking collectives, shards(): attention = lax.all_gather(own_attention, 'grp', axis=1, tiled=True)  28.5 us
    all_to_all x1, starting transfers between devices, shards(): lax.all_to_all(outbound, 'req', split_axis=0, concat_axis=0, tiled=True)  16.8 us
    all_to_all x1, starting transfers between devices, shards(): lax.all_to_all(jnp.broadcast_to(mid_owned[None], (groups,) + mid_owned.sh...  12.5 us
    all_to_all x1, starting transfers between devices, shards(): summed = jnp.sum(lax.all_to_all(partial, 'req', 0, 0, tiled=False), axis=0)  11 us
    all_to_all x1, waiting for transfers between devices, shards(): received = lax.all_to_all(parcel, 'grp', 0, 0, tiled=False)  10.9 us
    all_to_all x1, starting transfers between devices, shards(): received = lax.all_to_all(parcel, 'grp', 0, 0, tiled=False)  8.38 us
    all_to_all x1, waiting for transfers between devices, shards(): lax.all_to_all(outbound, 'req', split_axis=0, concat_axis=0, tiled=True)  7.77 us
    unnamed x29, local copies, waits for them, and re-layouts  4.87 us
  transfers between devices with their start and end apart: 4, of which 4 were waited for; matrix products, arithmetic and copies ran while one was open for 15% of the time, Pallas kernels for 0%

commit v1 on v0

--- a/solution.py
+++ b/solution.py
@@ -123,7 +123,25 @@
         + new_weight[..., None] * own_value.astype(jnp.float32)[:, None, :]
     )
     own_attention = (mixed / total[..., None]).astype(jnp.bfloat16).reshape(rows, mixed_width)
-    attention = lax.all_gather(own_attention, "grp", axis=1, tiled=True)
+    size, here, rows_2 = (lax.axis_size("grp"), lax.axis_index("grp"), own_attention.shape[1])
+    ahead = [(i, (i + 1) % size) for i in range(size)]
+    left = [(i, (i - 1) % size) for i in range(size)]
+    out = jnp.zeros(
+        (*own_attention.shape[:1], size * rows_2, *own_attention.shape[1 + 1 :]),
+        own_attention.dtype,
+    )
+    out = lax.dynamic_update_slice_in_dim(out, own_attention, here * rows_2, axis=1)
+    from_left = from_right = own_attention
+    middle = size // 2
+    for step in range(1, middle + 1):
+        from_left = lax.ppermute(from_left, "grp", ahead)
+        out = lax.dynamic_update_slice_in_dim(out, from_left, (here - step) % size * rows_2, axis=1)
+        if step < size - middle:
+            from_right = lax.ppermute(from_right, "grp", left)
+            out = lax.dynamic_update_slice_in_dim(
+                out, from_right, (here + step) % size * rows_2, axis=1
+            )
+    attention = out
     page_slot = page_slot_table[request_index, lengths // page_size]
     offset = lengths % page_size
     mine = offset // slot_tokens == group_index

time: 160 us -> 182 us (1.14)
  the two profiles are of different devices: /device:TPU:1 before, /device:TPU:2 now
where the time goes in v1:
time: 182 us; the launch traced here: 181 us
  starting transfers between devices  87.2 us (48%)
  local copies, waits for them, and re-layouts  38.8 us (21%)
  waiting for transfers between devices  33.9 us (19%)
  other arithmetic  16.2 us (9%)
  matrix products  3.03 us (2%)
    ppermute x7, starting transfers between devices, shards(): from_right = lax.ppermute(from_right, 'grp', left)  34.9 us
    all_to_all x1, waiting for transfers between devices, shards(): received = lax.all_to_all(parcel, 'grp', 0, 0, tiled=False)  18.3 us
    ppermute x8, starting transfers between devices, shards(): from_left = lax.ppermute(from_left, 'grp', ahead)  17.7 us
    all_to_all x1, starting transfers between devices, shards(): lax.all_to_all(jnp.broadcast_to(mid_owned[None], (groups,) + mid_owned.sh...  12.9 us
    all_to_all x1, waiting for transfers between devices, shards(): lax.all_to_all(jnp.broadcast_to(mid_owned[None], (groups,) + mid_owned.sh...  11.9 us
    all_to_all x1, starting transfers between devices, shards(): summed = jnp.sum(lax.all_to_all(partial, 'req', 0, 0, tiled=False), axis=0)  10.1 us
    all_to_all x1, starting transfers between devices, shards(): lax.all_to_all(outbound, 'req', split_axis=0, concat_axis=0, tiled=True)  7.33 us
    dynamic_update_slice x8, local copies, waits for them, and re-layouts, shards(): lax.dynamic_update_slice_in_dim(out, from_left, (here - step) % size * ro...  5.54 us
  transfers between devices with their start and end apart: 19, of which 3 were waited for; matrix products, arithmetic and copies ran while one was open for 19% of the time, Pallas kernels for 0%

profile of v1, /device:TPU:2, one launch (start us, length us, event | category | flops | bytes accessed | tf_op | source)
XLA Modules:
  0.0 180.5 jit_solution(752614731723997810)
XLA Ops:
  0.7 1.5 copy.107
  2.8 1.1 slice.84
  4.1 0.8 fusion.11
  4.9 1.0 copy.63
  5.8 1.3 multiply_reduce_fusion
  7.2 0.7 pad_maximum_fusion.1
  7.9 1.8 copy.43
  9.7 10.1 %all-to-all-start = ((f32[32,8,256]{2,1,0:T(8,128)}), f32[32,8,256]{2,1,0:T(8,128)}, u32[]{:S(2)}, u32[]{:S(2)}) async-start(f32[32,8,256]{2,1,0:T(8,128)} %bitcast.117), calls=%async_computation | async-start | bytes 524288 | tf_op jit(solution)/shard_map/all_to_all | solution.py:55
  19.9 1.8 gather_fusion
  21.6 1.3 fusion.45
  23.5 1.0 fusion.5
  24.8 0.7 copy.41
  25.5 1.7 reshape.115
  27.2 1.8 copy.44
  29.2 0.9 copy.45
  30.3 1.2 gather_fusion.2
  31.5 1.0 reduce_sum.48
  32.5 0.6 broadcast_in_dim.48
  33.1 12.9 %all-to-all-start.1 = ((bf16[16,8,128]{2,1,0:T(8,128)(2,1)}), bf16[16,8,128]{2,1,0:T(8,128)(2,1)}, u32[]{:S(2)}, u32[]{:S(2)}) async-start(bf16[16,8,128]{2,1,0:T(8,128)(2,1)} %broadcast_in_dim.48), calls=%async_computation.1 | async-start | bytes 65536 | tf_op jit(solution)/shard_map/all_to_all | solution.py:60
  46.0 0.7 fusion.37
  46.7 11.9 %all-to-all-done.1 = bf16[16,8,128]{2,1,0:T(8,128)(2,1)} async-done(((bf16[16,8,128]{2,1,0:T(8,128)(2,1)}), bf16[16,8,128]{2,1,0:T(8,128)(2,1)}, u32[]{:S(2)}, u32[]{:S(2)}) %all-to-all-start.1) | async-done | bytes 32800 | tf_op jit(solution)/shard_map/all_to_all | solution.py:60
  58.6 1.3 gather_fusion.1
  60.0 1.0 fusion.20
  61.1 0.7 fusion.23
  61.8 1.8 %maximum_bitcast_fusion = f32[16,8,648]{2,1,0:T(8,128)} fusion(f32[8,16,128]{2,0,1:T(8,128)S(1)} %broadcast_in_dim.49, f32[8,16,4]{2,0,1:T(8,128)S(1)} %copy.46, f32[8,16,4]{2,0,1:T(8,128)S(1)} %copy.45, f32[8,16,512]{2,0,1:T(8,128)} %copy.44), kind=kLoop, calls=%fused_computation.22 | loop fusion | flops 248832 | bytes 663552 | tf_op jit(solution)/shard_map/transpose | solution.py:96
  63.6 4.3 %all-to-all-start.2 = ((f32[16,8,648]{2,1,0:T(8,128)}), f32[16,8,648]{2,1,0:T(8,128)}, u32[]{:S(2)}, u32[]{:S(2)}) async-start(f32[16,8,648]{2,1,0:T(8,128)} %maximum_bitcast_fusion), calls=%async_computation.2 | async-start | bytes 786432 | tf_op jit(solution)/shard_map/all_to_all | solution.py:97
  68.2 0.6 gather_fusion.3
  70.7 0.7 dynamic-slice_bitcast_fusion
  72.1 18.3 %all-to-all-done.2 = f32[16,8,648]{2,1,0:T(8,128)} async-done(((f32[16,8,648]{2,1,0:T(8,128)}), f32[16,8,648]{2,1,0:T(8,128)}, u32[]{:S(2)}, u32[]{:S(2)}) %all-to-all-start.2) | async-done | bytes 331808 | tf_op jit(solution)/shard_map/all_to_all | solution.py:97
  90.3 1.0 fusion.14
  91.3 0.6 slice_bitcast_fusion.3
  92.7 0.9 slice_reduce_fusion
  93.5 1.0 fusion.13
  94.9 1.1 fusion.6
  96.0 1.4 constant_dynamic-update-slice_fusion.15
  97.4 4.4 %collective-permute-start = (bf16[8,512]{1,0:T(8,128)(2,1)}, bf16[8,512]{1,0:T(8,128)(2,1)}, u32[]{:S(2)}, u32[]{:S(2)}) collective-permute-start(bf16[8,512]{1,0:T(8,128)(2,1)} %get-tuple-element.3), channel_id=1, source_target_pairs={{0,1},{1,2},{2,3},{3,4},{4,5},{5,6},{6,7},{7,8},{8,9},{9,10},{10,1... | collective-permute-start | bytes 24584 | tf_op jit(solution)/shard_map/ppermute | solution.py:137
  101.7 4.1 %collective-permute-start.1 = (bf16[8,512]{1,0:T(8,128)(2,1)}, bf16[8,512]{1,0:T(8,128)(2,1)S(1)}, u32[]{:S(2)}, u32[]{:S(2)}) collective-permute-start(bf16[8,512]{1,0:T(8,128)(2,1)} %get-tuple-element.3), channel_id=1, source_target_pairs={{0,15},{1,0},{2,1},{3,2},{4,3},{5,4},{6,5},{7,6},{8,7},{9,8},{10,9... | collective-permute-start | bytes 24584 | tf_op jit(solution)/shard_map/ppermute | solution.py:140
  105.8 0.7 copy_bitcast_fusion.5
  106.6 0.7 maximum_select_fusion
  107.3 0.8 scatter_fusion
  108.1 1.2 slice_bitcast_fusion
  109.3 0.7 gather_fusion.5
  110.0 0.7 broadcast.243
  110.7 3.6 %scatter_fusion.1 = bf16[32,2,2,8,128]{4,3,2,1,0:T(8,128)(2,1)} fusion(bf16[32,2,2,8,128]{4,3,2,1,0:T(8,128)(2,1)} %broadcast.243, s32[32]{0:T(128)S(1)} %fusion.39, bf16[32,2,8,128]{3,2,1,0:T(8,128)(2,1)S(1)} %gather_fusion.5), kind=kCustom, calls=%fused_computation.7 | custom fusion | bytes 393472 | tf_op jit(solution)/shard_map/scatter | solution.py:164
  114.3 7.3 %all-to-all-start.3 = ((bf16[32,2,1,2,8,128]{5,4,3,1,2,0:T(8,128)(2,1)}), bf16[32,2,1,2,8,128]{5,4,3,1,2,0:T(8,128)(2,1)S(1)}, u32[]{:S(2)}, u32[]{:S(2)}) async-start(bf16[32,2,1,2,8,128]{5,4,3,1,2,0:T(8,128)(2,1)} %bitcast.41), calls=%async_computation.3 | async-start | bytes 524288 | tf_op jit(solution)/shard_map/all_to_all | solution.py:166
  121.6 1.9 %collective-permute-start.2 = (bf16[8,512]{1,0:T(8,128)(2,1)}, bf16[8,512]{1,0:T(8,128)(2,1)S(1)}, u32[]{:S(2)}, u32[]{:S(2)}) collective-permute-start(bf16[8,512]{1,0:T(8,128)(2,1)} %collective-permute-done), channel_id=1, source_target_pairs={{0,1},{1,2},{2,3},{3,4},{4,5},{5,6},{6,7},{7,8},{8,9},{9,10},{10,1... | collective-permute-start | bytes 24584 | tf_op jit(solution)/shard_map/ppermute | solution.py:137
  123.6 5.1 %collective-permute-start.3 = (bf16[8,512]{1,0:T(8,128)(2,1)S(1)}, bf16[8,512]{1,0:T(8,128)(2,1)S(1)}, u32[]{:S(2)}, u32[]{:S(2)}) collective-permute-start(bf16[8,512]{1,0:T(8,128)(2,1)S(1)} %collective-permute-done.1), channel_id=1, source_target_pairs={{0,15},{1,0},{2,1},{3,2},{4,3},{5,4},{6,5},{7,6},{8,7},{9,8},{10,9... | collective-permute-start | bytes 24584 | tf_op jit(solution)/shard_map/ppermute | solution.py:140
  128.7 1.3 constant_dynamic-update-slice_fusion.14
  130.6 1.9 %collective-permute-start.4 = (bf16[8,512]{1,0:T(8,128)(2,1)S(1)}, bf16[8,512]{1,0:T(8,128)(2,1)S(1)}, u32[]{:S(2)}, u32[]{:S(2)}) collective-permute-start(bf16[8,512]{1,0:T(8,128)(2,1)S(1)} %collective-permute-done.2), channel_id=1, source_target_pairs={{0,1},{1,2},{2,3},{3,4},{4,5},{5,6},{6,7},{7,8},{8,9},{9,10},{10,1... | collective-permute-start | bytes 24584 | tf_op jit(solution)/shard_map/ppermute | solution.py:137
  132.5 5.1 %collective-permute-start.5 = (bf16[8,512]{1,0:T(8,128)(2,1)S(1)}, bf16[8,512]{1,0:T(8,128)(2,1)S(1)}, u32[]{:S(2)}, u32[]{:S(2)}) collective-permute-start(bf16[8,512]{1,0:T(8,128)(2,1)S(1)} %collective-permute-done.3), channel_id=1, source_target_pairs={{0,15},{1,0},{2,1},{3,2},{4,3},{5,4},{6,5},{7,6},{8,7},{9,8},{10,9... | collective-permute-start | bytes 24584 | tf_op jit(solution)/shard_map/ppermute | solution.py:140
  138.9 1.9 %collective-permute-start.6 = (bf16[8,512]{1,0:T(8,128)(2,1)S(1)}, bf16[8,512]{1,0:T(8,128)(2,1)S(1)}, u32[]{:S(2)}, u32[]{:S(2)}) collective-permute-start(bf16[8,512]{1,0:T(8,128)(2,1)S(1)} %collective-permute-done.4), channel_id=1, source_target_pairs={{0,1},{1,2},{2,3},{3,4},{4,5},{5,6},{6,7},{7,8},{8,9},{9,10},{10,1... | collective-permute-start | bytes 24584 | tf_op jit(solution)/shard_map/ppermute | solution.py:137
  140.8 5.1 %collective-permute-start.7 = (bf16[8,512]{1,0:T(8,128)(2,1)S(1)}, bf16[8,512]{1,0:T(8,128)(2,1)S(1)}, u32[]{:S(2)}, u32[]{:S(2)}) collective-permute-start(bf16[8,512]{1,0:T(8,128)(2,1)S(1)} %collective-permute-done.5), channel_id=1, source_target_pairs={{0,15},{1,0},{2,1},{3,2},{4,3},{5,4},{6,5},{7,6},{8,7},{9,8},{10,9... | collective-permute-start | bytes 24584 | tf_op jit(solution)/shard_map/ppermute | solution.py:140
  147.2 1.9 %collective-permute-start.8 = (bf16[8,512]{1,0:T(8,128)(2,1)S(1)}, bf16[8,512]{1,0:T(8,128)(2,1)S(1)}, u32[]{:S(2)}, u32[]{:S(2)}) collective-permute-start(bf16[8,512]{1,0:T(8,128)(2,1)S(1)} %collective-permute-done.6), channel_id=1, source_target_pairs={{0,1},{1,2},{2,3},{3,4},{4,5},{5,6},{6,7},{7,8},{8,9},{9,10},{10,1... | collective-permute-start | bytes 24584 | tf_op jit(solution)/shard_map/ppermute | solution.py:137
  149.1 5.1 %collective-permute-start.9 = (bf16[8,512]{1,0:T(8,128)(2,1)S(1)}, bf16[8,512]{1,0:T(8,128)(2,1)S(1)}, u32[]{:S(2)}, u32[]{:S(2)}) collective-permute-start(bf16[8,512]{1,0:T(8,128)(2,1)S(1)} %collective-permute-done.7), channel_id=1, source_target_pairs={{0,15},{1,0},{2,1},{3,2},{4,3},{5,4},{6,5},{7,6},{8,7},{9,8},{10,9... | collective-permute-start | bytes 24584 | tf_op jit(solution)/shard_map/ppermute | solution.py:140
  154.2 0.6 constant_dynamic-update-slice_fusion.8
  155.4 1.9 %collective-permute-start.10 = (bf16[8,512]{1,0:T(8,128)(2,1)S(1)}, bf16[8,512]{1,0:T(8,128)(2,1)S(1)}, u32[]{:S(2)}, u32[]{:S(2)}) collective-permute-start(bf16[8,512]{1,0:T(8,128)(2,1)S(1)} %collective-permute-done.8), channel_id=1, source_target_pairs={{0,1},{1,2},{2,3},{3,4},{4,5},{5,6},{6,7},{7,8},{8,9},{9,10},{10,1... | collective-permute-start | bytes 24584 | tf_op jit(solution)/shard_map/ppermute | solution.py:137
  157.4 5.1 %collective-permute-start.11 = (bf16[8,512]{1,0:T(8,128)(2,1)S(1)}, bf16[8,512]{1,0:T(8,128)(2,1)S(1)}, u32[]{:S(2)}, u32[]{:S(2)}) collective-permute-start(bf16[8,512]{1,0:T(8,128)(2,1)S(1)} %collective-permute-done.9), channel_id=1, source_target_pairs={{0,15},{1,0},{2,1},{3,2},{4,3},{5,4},{6,5},{7,6},{8,7},{9,8},{10,9... | collective-permute-start | bytes 24584 | tf_op jit(solution)/shard_map/ppermute | solution.py:140
  162.5 0.6 constant_dynamic-update-slice_fusion.6
  163.7 1.9 %collective-permute-start.12 = (bf16[8,512]{1,0:T(8,128)(2,1)S(1)}, bf16[8,512]{1,0:T(8,128)(2,1)S(1)}, u32[]{:S(2)}, u32[]{:S(2)}) collective-permute-start(bf16[8,512]{1,0:T(8,128)(2,1)S(1)} %collective-permute-done.10), channel_id=1, source_target_pairs={{0,1},{1,2},{2,3},{3,4},{4,5},{5,6},{6,7},{7,8},{8,9},{9,10},{10,1... | collective-permute-start | bytes 24584 | tf_op jit(solution)/shard_map/ppermute | solution.py:137
  165.6 5.1 %collective-permute-start.13 = (bf16[8,512]{1,0:T(8,128)(2,1)S(1)}, bf16[8,512]{1,0:T(8,128)(2,1)S(1)}, u32[]{:S(2)}, u32[]{:S(2)}) collective-permute-start(bf16[8,512]{1,0:T(8,128)(2,1)S(1)} %collective-permute-done.11), channel_id=1, source_target_pairs={{0,15},{1,0},{2,1},{3,2},{4,3},{5,4},{6,5},{7,6},{8,7},{9,8},{10,9... | collective-permute-start | bytes 24584 | tf_op jit(solution)/shard_map/ppermute | solution.py:140
  170.8 0.6 constant_dynamic-update-slice_fusion.4
  172.0 1.9 %collective-permute-start.14 = (bf16[8,512]{1,0:T(8,128)(2,1)S(1)}, bf16[8,512]{1,0:T(8,128)(2,1)S(1)}, u32[]{:S(2)}, u32[]{:S(2)}) collective-permute-start(bf16[8,512]{1,0:T(8,128)(2,1)S(1)} %collective-permute-done.12), channel_id=1, source_target_pairs={{0,1},{1,2},{2,3},{3,4},{4,5},{5,6},{6,7},{7,8},{8,9},{9,10},{10,1... | collective-permute-start | bytes 24584 | tf_op jit(solution)/shard_map/ppermute | solution.py:137
  175.1 3.6 %collective-permute-done.14 = bf16[8,512]{1,0:T(8,128)(2,1)S(1)} collective-permute-done((bf16[8,512]{1,0:T(8,128)(2,1)S(1)}, bf16[8,512]{1,0:T(8,128)(2,1)S(1)}, u32[]{:S(2)}, u32[]{:S(2)}) %collective-permute-start.14) | collective-permute-done | bytes 8224 | tf_op jit(solution)/shard_map/ppermute | solution.py:137
  179.3 1.2 pad_maximum_fusion
  (92 shorter events, 12.3 us)
Async XLA Ops:
  0.6 29.6 %copy-start = (bf16[128,64,128]{2,1,0:T(8,128)(2,1)S(1)}, bf16[128,64,128]{2,1,0:T(8,128)(2,1)}, u32[]{:S(2)}) copy-start(bf16[128,64,128]{2,1,0:T(8,128)(2,1)} %param.14) | copy-start | bytes 6291460
  0.6 1.7 copy-start.6
  0.7 1.7 copy-start.7
  0.7 1.6 copy-start.4
  2.8 1.4 copy-start.2
  2.8 1.4 copy-start.9
  4.1 3.1 %slice-start = ((f32[256,1152]{0,1:T(8,128)}), f32[256,128]{0,1:T(8,128)S(1)}, s32[]{:S(2)}) async-start(f32[256,1152]{0,1:T(8,128)} %copy-done.2), calls=%async_computation.4 | async-start | bytes 262144 | tf_op jit(solution)/shard_map/slice | solution.py:47
  5.8 13.9 %copy-start.1 = (s32[8,32]{1,0:T(8,128)S(1)}, s32[8,32]{1,0:T(8,128)}, u32[]{:S(2)}) copy-start(s32[8,32]{1,0:T(8,128)} %param.19) | copy-start | bytes 3076
  9.7 21.8 %all-to-all-start = ((f32[32,8,256]{2,1,0:T(8,128)}), f32[32,8,256]{2,1,0:T(8,128)}, u32[]{:S(2)}, u32[]{:S(2)}) async-start(f32[32,8,256]{2,1,0:T(8,128)} %bitcast.117), calls=%async_computation | async-start | bytes 524288 | tf_op jit(solution)/shard_map/all_to_all | solution.py:55
  21.6 1.3 copy-start.11
  21.6 1.4 copy-start.10
  32.5 0.6 copy-start.8
  33.1 25.5 %all-to-all-start.1 = ((bf16[16,8,128]{2,1,0:T(8,128)(2,1)}), bf16[16,8,128]{2,1,0:T(8,128)(2,1)}, u32[]{:S(2)}, u32[]{:S(2)}) async-start(bf16[16,8,128]{2,1,0:T(8,128)(2,1)} %broadcast_in_dim.48), calls=%async_computation.1 | async-start | bytes 65536 | tf_op jit(solution)/shard_map/all_to_all | solution.py:60
  61.8 9.8 %copy-start.12 = (s32[8]{0:T(128)S(1)}, s32[8]{0:T(128)}, u32[]{:S(2)}) copy-start(s32[8]{0:T(128)} %param.18) | copy-start | bytes 100
  63.6 6.4 %copy-start.13 = (s32[32]{0:T(128)S(1)}, s32[32]{0:T(128)}, u32[]{:S(2)}) copy-start(s32[32]{0:T(128)} %param.20) | copy-start | bytes 388
  63.6 7.8 %copy-start.14 = (s32[32,1]{0,1:T(1,128)S(1)}, s32[32,1]{0,1:T(1,128)}, u32[]{:S(2)}) copy-start(s32[32,1]{0,1:T(1,128)} %param.21) | copy-start | bytes 388
  63.6 26.7 %all-to-all-start.2 = ((f32[16,8,648]{2,1,0:T(8,128)}), f32[16,8,648]{2,1,0:T(8,128)}, u32[]{:S(2)}, u32[]{:S(2)}) async-start(f32[16,8,648]{2,1,0:T(8,128)} %maximum_bitcast_fusion), calls=%async_computation.2 | async-start | bytes 786432 | tf_op jit(solution)/shard_map/all_to_all | solution.py:97
  97.4 9.9 %copy-start.5 = (bf16[8,8192]{1,0:T(8,128)(2,1)}, bf16[8,8192]{1,0:T(8,128)(2,1)S(1)}, u32[]{:S(2)}) copy-start(bf16[8,8192]{1,0:T(8,128)(2,1)S(1)} %get-tuple-element.2) | copy-start | bytes 393220
  97.4 24.3 %collective-permute-start = (bf16[8,512]{1,0:T(8,128)(2,1)}, bf16[8,512]{1,0:T(8,128)(2,1)}, u32[]{:S(2)}, u32[]{:S(2)}) collective-permute-start(bf16[8,512]{1,0:T(8,128)(2,1)} %get-tuple-element.3), channel_id=1, source_target_pairs={{0,1},{1,2},{2,3},{3,4},{4,5},{5,6},{6,7},{7,8},{8,9},{9,10},{10,1... | collective-permute-start | bytes 24584 | tf_op jit(solution)/shard_map/ppermute | solution.py:137
  101.7 21.8 %collective-permute-start.1 = (bf16[8,512]{1,0:T(8,128)(2,1)}, bf16[8,512]{1,0:T(8,128)(2,1)S(1)}, u32[]{:S(2)}, u32[]{:S(2)}) collective-permute-start(bf16[8,512]{1,0:T(8,128)(2,1)} %get-tuple-element.3), channel_id=1, source_target_pairs={{0,15},{1,0},{2,1},{3,2},{4,3},{5,4},{6,5},{7,6},{8,7},{9,8},{10,9... | collective-permute-start | bytes 24584 | tf_op jit(solution)/shard_map/ppermute | solution.py:140
  110.0 69.4 %copy-start.3 = (bf16[256,1,2,8,128]{4,3,2,1,0:T(8,128)(2,1)S(1)}, bf16[256,1,2,8,128]{4,3,2,1,0:T(8,128)(2,1)}, u32[]{:S(2)}) copy-start(bf16[256,1,2,8,128]{4,3,2,1,0:T(8,128)(2,1)} %slice_bitcast_fusion) | copy-start | bytes 3145732
  114.3 65.1 %all-to-all-start.3 = ((bf16[32,2,1,2,8,128]{5,4,3,1,2,0:T(8,128)(2,1)}), bf16[32,2,1,2,8,128]{5,4,3,1,2,0:T(8,128)(2,1)S(1)}, u32[]{:S(2)}, u32[]{:S(2)}) async-start(bf16[32,2,1,2,8,128]{5,4,3,1,2,0:T(8,128)(2,1)} %bitcast.41), calls=%async_computation.3 | async-start | bytes 524288 | tf_op jit(solution)/shard_map/all_to_all | solution.py:166
  121.6 9.0 %collective-permute-start.2 = (bf16[8,512]{1,0:T(8,128)(2,1)}, bf16[8,512]{1,0:T(8,128)(2,1)S(1)}, u32[]{:S(2)}, u32[]{:S(2)}) collective-permute-start(bf16[8,512]{1,0:T(8,128)(2,1)} %collective-permute-done), channel_id=1, source_target_pairs={{0,1},{1,2},{2,3},{3,4},{4,5},{5,6},{6,7},{7,8},{8,9},{9,10},{10,1... | collective-permute-start | bytes 24584 | tf_op jit(solution)/shard_map/ppermute | solution.py:137
  123.6 9.0 %collective-permute-start.3 = (bf16[8,512]{1,0:T(8,128)(2,1)S(1)}, bf16[8,512]{1,0:T(8,128)(2,1)S(1)}, u32[]{:S(2)}, u32[]{:S(2)}) collective-permute-start(bf16[8,512]{1,0:T(8,128)(2,1)S(1)} %collective-permute-done.1), channel_id=1, source_target_pairs={{0,15},{1,0},{2,1},{3,2},{4,3},{5,4},{6,5},{7,6},{8,7},{9,8},{10,9... | collective-permute-start | bytes 24584 | tf_op jit(solution)/shard_map/ppermute | solution.py:140
  130.6 8.3 %collective-permute-start.4 = (bf16[8,512]{1,0:T(8,128)(2,1)S(1)}, bf16[8,512]{1,0:T(8,128)(2,1)S(1)}, u32[]{:S(2)}, u32[]{:S(2)}) collective-permute-start(bf16[8,512]{1,0:T(8,128)(2,1)S(1)} %collective-permute-done.2), channel_id=1, source_target_pairs={{0,1},{1,2},{2,3},{3,4},{4,5},{5,6},{6,7},{7,8},{8,9},{9,10},{10,1... | collective-permute-start | bytes 24584 | tf_op jit(solution)/shard_map/ppermute | solution.py:137
  132.5 8.3 %collective-permute-start.5 = (bf16[8,512]{1,0:T(8,128)(2,1)S(1)}, bf16[8,512]{1,0:T(8,128)(2,1)S(1)}, u32[]{:S(2)}, u32[]{:S(2)}) collective-permute-start(bf16[8,512]{1,0:T(8,128)(2,1)S(1)} %collective-permute-done.3), channel_id=1, source_target_pairs={{0,15},{1,0},{2,1},{3,2},{4,3},{5,4},{6,5},{7,6},{8,7},{9,8},{10,9... | collective-permute-start | bytes 24584 | tf_op jit(solution)/shard_map/ppermute | solution.py:140
  138.9 8.3 %collective-permute-start.6 = (bf16[8,512]{1,0:T(8,128)(2,1)S(1)}, bf16[8,512]{1,0:T(8,128)(2,1)S(1)}, u32[]{:S(2)}, u32[]{:S(2)}) collective-permute-start(bf16[8,512]{1,0:T(8,128)(2,1)S(1)} %collective-permute-done.4), channel_id=1, source_target_pairs={{0,1},{1,2},{2,3},{3,4},{4,5},{5,6},{6,7},{7,8},{8,9},{9,10},{10,1... | collective-permute-start | bytes 24584 | tf_op jit(solution)/shard_map/ppermute | solution.py:137
  140.8 8.3 %collective-permute-start.7 = (bf16[8,512]{1,0:T(8,128)(2,1)S(1)}, bf16[8,512]{1,0:T(8,128)(2,1)S(1)}, u32[]{:S(2)}, u32[]{:S(2)}) collective-permute-start(bf16[8,512]{1,0:T(8,128)(2,1)S(1)} %collective-permute-done.5), channel_id=1, source_target_pairs={{0,15},{1,0},{2,1},{3,2},{4,3},{5,4},{6,5},{7,6},{8,7},{9,8},{10,9... | collective-permute-start | bytes 24584 | tf_op jit(solution)/shard_map/ppermute | solution.py:140
  147.2 8.3 %collective-permute-start.8 = (bf16[8,512]{1,0:T(8,128)(2,1)S(1)}, bf16[8,512]{1,0:T(8,128)(2,1)S(1)}, u32[]{:S(2)}, u32[]{:S(2)}) collective-permute-start(bf16[8,512]{1,0:T(8,128)(2,1)S(1)} %collective-permute-done.6), channel_id=1, source_target_pairs={{0,1},{1,2},{2,3},{3,4},{4,5},{5,6},{6,7},{7,8},{8,9},{9,10},{10,1... | collective-permute-start | bytes 24584 | tf_op jit(solution)/shard_map/ppermute | solution.py:137
  149.1 8.3 %collective-permute-start.9 = (bf16[8,512]{1,0:T(8,128)(2,1)S(1)}, bf16[8,512]{1,0:T(8,128)(2,1)S(1)}, u32[]{:S(2)}, u32[]{:S(2)}) collective-permute-start(bf16[8,512]{1,0:T(8,128)(2,1)S(1)} %collective-permute-done.7), channel_id=1, source_target_pairs={{0,15},{1,0},{2,1},{3,2},{4,3},{5,4},{6,5},{7,6},{8,7},{9,8},{10,9... | collective-permute-start | bytes 24584 | tf_op jit(solution)/shard_map/ppermute | solution.py:140
  155.4 8.3 %collective-permute-start.10 = (bf16[8,512]{1,0:T(8,128)(2,1)S(1)}, bf16[8,512]{1,0:T(8,128)(2,1)S(1)}, u32[]{:S(2)}, u32[]{:S(2)}) collective-permute-start(bf16[8,512]{1,0:T(8,128)(2,1)S(1)} %collective-permute-done.8), channel_id=1, source_target_pairs={{0,1},{1,2},{2,3},{3,4},{4,5},{5,6},{6,7},{7,8},{8,9},{9,10},{10,1... | collective-permute-start | bytes 24584 | tf_op jit(solution)/shard_map/ppermute | solution.py:137
  157.4 8.3 %collective-permute-start.11 = (bf16[8,512]{1,0:T(8,128)(2,1)S(1)}, bf16[8,512]{1,0:T(8,128)(2,1)S(1)}, u32[]{:S(2)}, u32[]{:S(2)}) collective-permute-start(bf16[8,512]{1,0:T(8,128)(2,1)S(1)} %collective-permute-done.9), channel_id=1, source_target_pairs={{0,15},{1,0},{2,1},{3,2},{4,3},{5,4},{6,5},{7,6},{8,7},{9,8},{10,9... | collective-permute-start | bytes 24584 | tf_op jit(solution)/shard_map/ppermute | solution.py:140
  163.7 8.3 %collective-permute-start.12 = (bf16[8,512]{1,0:T(8,128)(2,1)S(1)}, bf16[8,512]{1,0:T(8,128)(2,1)S(1)}, u32[]{:S(2)}, u32[]{:S(2)}) collective-permute-start(bf16[8,512]{1,0:T(8,128)(2,1)S(1)} %collective-permute-done.10), channel_id=1, source_target_pairs={{0,1},{1,2},{2,3},{3,4},{4,5},{5,6},{6,7},{7,8},{8,9},{9,10},{10,1... | collective-permute-start | bytes 24584 | tf_op jit(solution)/shard_map/ppermute | solution.py:137
  165.6 8.9 %collective-permute-start.13 = (bf16[8,512]{1,0:T(8,128)(2,1)S(1)}, bf16[8,512]{1,0:T(8,128)(2,1)S(1)}, u32[]{:S(2)}, u32[]{:S(2)}) collective-permute-start(bf16[8,512]{1,0:T(8,128)(2,1)S(1)} %collective-permute-done.11), channel_id=1, source_target_pairs={{0,15},{1,0},{2,1},{3,2},{4,3},{5,4},{6,5},{7,6},{8,7},{9,8},{10,9... | collective-permute-start | bytes 24584 | tf_op jit(solution)/shard_map/ppermute | solution.py:140
  172.0 6.7 %collective-permute-start.14 = (bf16[8,512]{1,0:T(8,128)(2,1)S(1)}, bf16[8,512]{1,0:T(8,128)(2,1)S(1)}, u32[]{:S(2)}, u32[]{:S(2)}) collective-permute-start(bf16[8,512]{1,0:T(8,128)(2,1)S(1)} %collective-permute-done.12), channel_id=1, source_target_pairs={{0,1},{1,2},{2,3},{3,4},{4,5},{5,6},{6,7},{7,8},{8,9},{9,10},{10,1... | collective-permute-start | bytes 24584 | tf_op jit(solution)/shard_map/ppermute | solution.py:137
